TPU v7x, 32 devices: a whole 2x2x4 slice. The times are simulated.
32 devices in a mesh: grp: 2 (over x), tile: 16 (over z, y, core).
Axes of the slice: x: 2, y: 2, z: 4, core: 2. Of those that a mesh axis runs over, the one named last changes fastest.
Arguments:
- latents: bfloat16 [384, 16, 8, 256], P(('grp', 'tile')), parts along dimension 0, may hold values from -6 to 6
- frame_counts: int32 [32], P('grp'), parts along dimension 0, may hold values from 1 to 12, 64 in all
- clip_order: int32 [32], P('grp'), parts along dimension 0, may hold values from 0 to 15, each once
- norm_scale: float32 [256], replicated, may hold values from 0.25 to 1.75
- norm_offset: float32 [256], replicated, may hold values from -3 to 3
- conv_weight: bfloat16 [3, 3, 3, 256, 256], replicated, may hold values from -0.078125 to 0.078125
- conv_bias: float32 [256], replicated, may hold values from -3 to 3
- out_scale: float32 [256], replicated, may hold values from 0.25 to 1.75
- out_offset: float32 [256], replicated, may hold values from -3 to 3
Outputs:
- block_out: bfloat16 [2, 1024, 8, 256], P(None, ('grp', 'tile')), parts along dimension 1
- normed: bfloat16 [2, 1024, 8, 256], P(None, ('grp', 'tile')), parts along dimension 1
There are 2 independent parts, one for each index of `grp`. A program takes and returns all parts, laid end to end along the dimension named above; an argument that names none is the same for every part. Nothing has to cross between parts.
Inputs may be any that keep to these rules, and one draw needn't show every extreme that they name: `frame_counts`: they sum to 64; the largest is exactly 12. `clip_order`: A permutation of the clips.
All inputs are finite; a program needn't handle non-finite values.
Results may differ from a plain program's by a relative error of at most 0.0057.
Values may be sent and summed in bfloat16 or wider, within the bound.
No kernel may reach another device: no remote copies, remote signals or barrier semaphores. Data moves between devices by JAX's collectives and lax.ppermute only.
A program may use at most 64 MiB of HBM per device.

v0:
```python
import jax
import jax.numpy as jnp
from jax import lax
from jax.sharding import PartitionSpec as P

GROUPS = 32
MEANF = 4
NRB = 8
eps = 1e-06


def normalize(values, frame_count, scaling, offsets):
    frames = values.shape[0]
    channels = values.shape[-1]
    grouped = values.reshape(frames, -1, GROUPS, channels // GROUPS)
    live_mask = (jnp.arange(frames) < frame_count).astype(jnp.float32)[:, None, None, None]
    members = frame_count.astype(jnp.float32) * grouped.shape[1] * grouped.shape[3]
    group_mean = jnp.sum(grouped * live_mask, axis=(0, 1, 3)) / members
    spread = (
        jnp.sum(grouped * grouped * live_mask, axis=(0, 1, 3)) / members - group_mean * group_mean
    )
    inverse = lax.rsqrt(spread + eps)
    normed = (grouped - group_mean[:, None]) * inverse[:, None] * scaling.reshape(
        GROUPS, -1
    ) + offsets.reshape(GROUPS, -1)
    return jax.nn.silu(normed).reshape(values.shape)


def convolve(stacked, kernel, offsets):
    tile_rows = stacked.shape[1] - 2
    columns = stacked.shape[3]
    channels = stacked.shape[4]
    padded = jnp.pad(stacked, ((0, 0), (0, 0), (0, 0), (1, 1), (0, 0)))
    tap_list = [
        padded[frame_lag, row_tap : row_tap + tile_rows, :, col_tap : col_tap + columns]
        for frame_lag in range(3)
        for row_tap in range(3)
        for col_tap in range(3)
    ]
    unfolded = jnp.concatenate(tap_list, axis=-1)
    result = jnp.dot(
        unfolded.reshape(-1, 27 * channels),
        kernel.reshape(27 * channels, -1),
        preferred_element_type=jnp.float32,
    )
    return (result + offsets).reshape(tile_rows, stacked.shape[2], columns, -1)


def local(
    latents,
    frame_counts,
    clip_order,
    norm_scale,
    norm_offset,
    conv_weight,
    conv_bias,
    out_scale,
    out_offset,
):
    devices = lax.axis_size("tile")
    device = lax.axis_index("tile")
    frames, frame_rows, columns, channels = latents.shape
    tile_rows = frame_rows // NRB
    own_tiles = frames * NRB
    capacity = (own_tiles + devices - 1) // devices
    slots_all = devices * capacity
    worker_tiles = MEANF * NRB
    positions = jnp.arange(frame_counts.shape[0], dtype=jnp.int32)
    chosen = clip_order[:, None] == positions[None, :]
    ordered = jnp.sum(jnp.where(chosen, frame_counts[None, :], 0), axis=1)
    starts = (jnp.cumsum(ordered) - ordered) * NRB
    own_start = jnp.sum(jnp.where(clip_order == device, starts, 0))
    own_count = jnp.sum(jnp.where(positions == device, frame_counts, 0))
    active = normalize(latents.astype(jnp.float32), own_count, norm_scale, norm_offset).astype(
        jnp.bfloat16
    )
    outgoing_slot = jnp.arange(slots_all, dtype=jnp.int32)
    target = outgoing_slot // capacity
    source_tile = outgoing_slot % capacity * devices + (target - own_start) % devices
    sendable = source_tile < own_count * NRB
    source_tile = jnp.minimum(source_tile, own_tiles - 1)
    local_slot = jnp.arange(worker_tiles, dtype=jnp.int32)
    tile_id = local_slot * devices + device
    placed = jnp.sum((starts[None, :] <= tile_id[:, None]).astype(jnp.int32), axis=1) - 1
    at_place = placed[:, None] == positions[None, :]
    clip_id = jnp.sum(jnp.where(at_place, clip_order[None, :], 0), axis=1)
    within = tile_id - jnp.sum(jnp.where(at_place, starts[None, :], 0), axis=1)
    take_from = clip_id * capacity + within // devices
    padded = jnp.pad(active, ((2, 0), (1, 1), (0, 0), (0, 0)))
    lagged = []
    for frame_lag in range(3):
        window = padded[frame_lag : frame_lag + frames]
        row_bands = [
            window[:, row_start : row_start + NRB * tile_rows : tile_rows]
            for row_start in range(tile_rows + 2)
        ]
        lagged.append(jnp.stack(row_bands, 0))
    pieces = jnp.stack(lagged, 0).reshape(3, tile_rows + 2, own_tiles, columns, channels)
    outgoing = jnp.where(
        sendable[None, None, :, None, None], jnp.take(pieces, source_tile, axis=2), 0
    )
    received = lax.all_to_all(outgoing, "tile", split_axis=2, concat_axis=2, tiled=True)
    stacked = jnp.take(received, take_from, axis=2)
    block_out = convolve(stacked, conv_weight, conv_bias).astype(jnp.bfloat16)
    per_group = channels // GROUPS
    grouped = block_out.astype(jnp.float32).reshape(
        tile_rows, worker_tiles, columns, GROUPS, per_group
    )
    first_sum = jnp.sum(grouped, axis=(0, 2, 4))
    second_sum = jnp.sum(grouped * grouped, axis=(0, 2, 4))
    belongs = (clip_id[:, None] == positions[None, :]).astype(jnp.float32)
    totals = lax.psum(
        (
            jnp.dot(belongs.T, first_sum, precision=lax.Precision.HIGHEST),
            jnp.dot(belongs.T, second_sum, precision=lax.Precision.HIGHEST),
        ),
        "tile",
    )
    members = frame_counts.astype(jnp.float32) * (frame_rows * columns * per_group)
    clip_mean = totals[0] / members[:, None]
    clip_spread = totals[1] / members[:, None] - clip_mean * clip_mean
    clip_inverse = lax.rsqrt(clip_spread + eps)
    tile_mean = jnp.dot(belongs, clip_mean, precision=lax.Precision.HIGHEST)
    tile_inverse = jnp.dot(belongs, clip_inverse, precision=lax.Precision.HIGHEST)
    normed = (grouped - tile_mean[None, :, None, :, None]) * tile_inverse[
        None, :, None, :, None
    ] * out_scale.reshape(GROUPS, per_group) + out_offset.reshape(GROUPS, per_group)
    normed = jax.nn.silu(normed).astype(jnp.bfloat16).reshape(block_out.shape)
    return (block_out, normed)


def solution(mesh):
    in_specs = (
        P(("grp", "tile"), None, None, None),
        P("grp"),
        P("grp"),
        P(),
        P(),
        P(),
        P(),
        P(),
        P(),
    )
    out_specs = (P(None, ("grp", "tile"), None, None), P(None, ("grp", "tile"), None, None))
    return jax.shard_map(local, mesh=mesh, in_specs=in_specs, out_specs=out_specs, check_vma=False)
```

profile of v0, /device:TPU:0, one launch (start us, length us, event | category | flops | bytes accessed | tf_op | source)
XLA Modules:
  0.0 250.5 jit_solution(12813425869111469504)
XLA Ops:
  0.6 1.0 select_reduce_fusion.2
  1.7 0.5 copy-done.4
  2.3 0.1 reduce.4
  2.4 2.0 fusion.32
  4.4 0.6 compare_convert_fusion
  5.5 1.2 fusion.39
  6.7 1.3 compare_and_fusion
  8.0 2.2 fusion.11
  10.3 0.8 reduce_sum.113
  11.0 1.4 reduce_sum.116
  12.4 0.6 reduce_sum.114
  13.0 0.8 reduce_sum.117
  13.9 1.2 add_rsqrt_fusion
  15.1 0.7 mul.182
  15.8 0.7 sub.107
  16.5 0.7 sub.108
  17.1 1.7 fusion.9
  18.9 0.2 pad_slice_fusion.20
  19.1 1.3 fusion.44
  20.3 1.2 fusion.46
  21.6 1.2 fusion.45
  23.3 0.7 broadcast_compare_fusion
  24.0 5.2 %maximum_maximum_fusion = bf16[3,4,96,8,256]{4,3,2,1,0:T(8,128)(2,1)} fusion(bf16[1,1,96,8,256]{4,3,2,1,0:T(8,128)(2,1)} %bitcast.72, bf16[1,1,96,8,256]{4,3,2,1,0:T(8,128)(2,1)} %bitcast.73, bf16[1,1,96,8,256]{4,3,2,1,0:T(8,128)(2,1)} %bitcast.74, bf16[1,1,96,8,256]{4,3,2,1,0:T(8,128)(2,1)} %bitcast.71, bf16[1,1,96,8,256]{4,3,2,1,0:T(8,128)(2,1)} %bitcast.76, ...), kind=kLoop, calls=%fused_computation.21 | loop fusion | flops 25952256 | bytes 9437184 | tf_op jit(solution)/shard_map/stack | solution.py:98
  29.2 5.9 %gather_fusion = bf16[96,3,4,8,256]{4,3,2,1,0:T(8,128)(2,1)} fusion(bf16[3,4,96,8,256]{4,3,2,1,0:T(8,128)(2,1)} %maximum_maximum_fusion, s32[1024]{0:T(1024)S(1)} %pad_clamp_fusion.1), kind=kCustom, calls=%fused_computation | custom fusion | bytes 9437568 | tf_op jit(solution)/shard_map/jit(_take)/gather | solution.py:100
  35.1 5.1 %select_bitcast_fusion = bf16[3,4,96,8,256]{4,3,1,0,2:T(8,128)(2,1)} fusion(bf16[96,3,4,8,256]{4,3,2,1,0:T(8,128)(2,1)} %gather_fusion, pred[96]{0:T(512)(128)(4,1)S(1)} %broadcast_compare_fusion, pred[96]{0:T(512)(128)(4,1)S(1)} %copy-done.5), kind=kLoop, calls=%fused_computation.22 | loop fusion | flops 4718592 | bytes 9437376 | tf_op jit(solution)/shard_map/jit(_where)/select_n | solution.py:99
  40.2 7.6 %all-to-all-start = ((bf16[3,4,96,8,256]{4,3,1,0,2:T(8,128)(2,1)}), bf16[3,4,96,8,256]{4,3,1,0,2:T(8,128)(2,1)}, u32[]{:S(2)}, u32[]{:S(2)}) async-start(bf16[3,4,96,8,256]{4,3,1,0,2:T(8,128)(2,1)} %select_bitcast_fusion), calls=%async_computation | async-start | bytes 9437184 | tf_op jit(solution)/shard_map/all_to_all | solution.py:102
  47.8 0.1 convert_reduce_fusion
  48.1 1.2 convert_multiply_fusion.2
  49.3 85.3 %all-to-all-done = bf16[3,4,96,8,256]{4,3,1,0,2:T(8,128)(2,1)} async-done(((bf16[3,4,96,8,256]{4,3,1,0,2:T(8,128)(2,1)}), bf16[3,4,96,8,256]{4,3,1,0,2:T(8,128)(2,1)}, u32[]{:S(2)}, u32[]{:S(2)}) %all-to-all-start) | async-done | bytes 4718624 | tf_op jit(solution)/shard_map/all_to_all | solution.py:102
  134.6 4.9 %copy.83 = bf16[3,4,96,8,256]{4,3,2,1,0:T(8,128)(2,1)} copy(bf16[3,4,96,8,256]{4,3,1,0,2:T(8,128)(2,1)} %all-to-all-done) | data formatting | bytes 9437184 | tf_op jit(solution)/shard_map/all_to_all | solution.py:102
  139.5 4.2 %gather_fusion.1 = bf16[32,3,4,8,256]{4,3,2,1,0:T(8,128)(2,1)} fusion(bf16[3,4,96,8,256]{4,3,2,1,0:T(8,128)(2,1)} %copy.83, s32[1024]{0:T(1024)S(1)} %pad_clamp_fusion), kind=kCustom, calls=%fused_computation.1 | custom fusion | bytes 3145856 | tf_op jit(solution)/shard_map/jit(_take)/gather | solution.py:103
  143.8 1.6 select_bitcast_fusion.1
  145.4 0.2 fusion.43
  145.6 1.2 pad_slice_fusion
  148.3 0.2 copy-done.7
  148.5 2.7 %fusion.12 = bf16[512,256]{1,0:T(8,128)(2,1)} fusion(bf16[512,6912]{1,0:T(8,128)(2,1)S(1)} %constant_dynamic-update-slice_fusion, bf16[6912,256]{1,0:T(8,128)(2,1)S(1)} %bitcast.66, f32[256]{0:T(256)S(1)} %copy-done.7), kind=kOutput, calls=%fused_computation.40 | convolution fusion | flops 1812201472 | bytes 10880000 | tf_op jit(solution)/shard_map/dot_general | solution.py:41
  151.2 7.0 %reshape.406 = f32[2,32,8,32,8]{4,3,2,1,0:T(8,128)} reshape(bf16[512,256]{1,0:T(8,128)(2,1)} %fusion.12) | data formatting | bytes 786432 | tf_op jit(solution)/shard_map/convert_element_type | solution.py:106
  158.2 5.0 %fusion.42 = (f32[32,32]{1,0:T(8,128)S(1)}, f32[32,32]{1,0:T(8,128)S(1)}) fusion(f32[2,32,8,32,8]{4,3,2,1,0:T(8,128)} %reshape.406), kind=kLoop, calls=%fused_computation.154 | loop fusion | flops 391168 | bytes 532480 | tf_op jit(solution)/shard_map/reduce_sum | solution.py:109
  163.2 0.3 fusion.16
  163.5 0.9 fusion.14
  164.4 77.8 %all-reduce.2 = (f32[16,32]{1,0:T(8,128)}, f32[16,32]{1,0:T(8,128)}) all-reduce(f32[16,32]{1,0:T(8,128)S(1)} %fusion.14, f32[16,32]{1,0:T(8,128)S(1)} %fusion.16), channel_id=1, replica_groups=mesh['grp'=2,'tile'=16] {'tile'}, use_global_device_ids=true, to_apply=%region_14.15 | all-reduce | flops 1024 | bytes 8192 | tf_op jit(solution)/shard_map/psum | solution.py:112
  242.2 1.0 fusion.15
  243.1 0.7 broadcast_bitcast_fusion.1
  243.8 1.6 copy.112
  245.4 1.0 fusion.13
  246.4 0.7 broadcast_bitcast_fusion
  247.1 1.6 copy.114
  248.7 1.9 multiply_convert_fusion
  (78 shorter events, 1.4 us)
Async XLA Ops:
  0.6 147.7 %copy-start = (bf16[3,3,3,256,256]{4,3,2,1,0:T(8,128)(2,1)S(1)}, bf16[3,3,3,256,256]{4,3,2,1,0:T(8,128)(2,1)}, u32[]{:S(2)}) copy-start(bf16[3,3,3,256,256]{4,3,2,1,0:T(8,128)(2,1)} %param.14) | copy-start | bytes 10616836
  1.7 0.5 copy-start.4
  19.1 3.7 %copy-start.6 = (s32[96]{0:T(128)S(1)}, s32[96]{0:T(128)}, u32[]{:S(2)}) copy-start(s32[96]{0:T(128)} %fusion.39) | copy-start | bytes 1156
  29.2 5.9 %copy-start.5 = (pred[96]{0:T(512)(128)(4,1)S(1)}, pred[96]{0:T(512)(128)(4,1)}, u32[]{:S(2)}) copy-start(pred[96]{0:T(512)(128)(4,1)} %compare_and_fusion) | copy-start | bytes 292
  40.2 7.6 %copy-start.3 = (s32[16]{0:T(128)S(1)}, s32[16]{0:T(128)}, u32[]{:S(2)}) copy-start(s32[16]{0:T(128)} %get-tuple-element.11) | copy-start | bytes 196
  40.2 7.7 %copy-start.2 = (s32[16]{0:T(128)S(1)}, s32[16]{0:T(128)}, u32[]{:S(2)}) copy-start(s32[16]{0:T(128)} %param.11) | copy-start | bytes 196
  40.2 94.4 %all-to-all-start = ((bf16[3,4,96,8,256]{4,3,1,0,2:T(8,128)(2,1)}), bf16[3,4,96,8,256]{4,3,1,0,2:T(8,128)(2,1)}, u32[]{:S(2)}, u32[]{:S(2)}) async-start(bf16[3,4,96,8,256]{4,3,1,0,2:T(8,128)(2,1)} %select_bitcast_fusion), calls=%async_computation | async-start | bytes 9437184 | tf_op jit(solution)/shard_map/all_to_all | solution.py:102
  48.0 115.2 %copy-start.1 = (s32[32]{0:T(128)}, s32[32]{0:T(128)S(1)}, u32[]{:S(2)}) copy-start(s32[32]{0:T(128)S(1)} %get-tuple-element.6) | copy-start | bytes 388
  147.8 0.7 copy-start.7
where the time goes:
time: 252 us; the launch traced here: 251 us
  waiting for transfers between devices  85.3 us (34%)
  blocking collectives  77.8 us (31%)
  local copies, waits for them, and re-layouts  37.9 us (15%)
  other arithmetic  33.9 us (13%)
  starting transfers between devices  7.56 us (3%)
  matrix products  5.83 us (2%)
    all_to_all x1, waiting for transfers between devices, local(): lax.all_to_all(outgoing, 'tile', split_axis=2, concat_axis=2, tiled=True)  85.3 us
    psum x1, blocking collectives, local(): lax.psum((jnp.dot(belongs.T, first_sum, precision=lax.Precision.HIGHEST),...  77.8 us
    all_to_all x1, starting transfers between devices, local(): lax.all_to_all(outgoing, 'tile', split_axis=2, concat_axis=2, tiled=True)  7.56 us
    convert_element_type x1, local copies, waits for them, and re-layouts, local(): block_out.astype(jnp.float32)  7 us
    gather x1, local copies, waits for them, and re-layouts, local(): jnp.take(pieces, source_tile, axis=2)  5.85 us
    another operation x1, other arithmetic, local(): jnp.stack(lagged, 0).reshape(3, tile_rows + 2, own_tiles, columns, channels)  5.21 us
    select_n x1, other arithmetic, local(): jnp.where(sendable[None, None, :, None, None], jnp.take(pieces, source_ti...  5.14 us
  transfers between devices with their start and end apart: 1, of which 1 were waited for; matrix products, arithmetic and copies ran while one was open for 1% of the time, Pallas kernels for 0%

commit v1 on v0

--- a/solution.py
+++ b/solution.py
@@ -7,6 +7,17 @@
 MEANF = 4
 NRB = 8
 eps = 1e-06
+
+
+def split_up(x, dim, size):
+    before, after = (x.shape[:dim], x.shape[dim + 1 :])
+    return jnp.moveaxis(x.reshape(*before, size, -1, *after), dim, 0)
+
+
+def laid_out(blocks, dim):
+    shape = list(blocks.shape[1:])
+    shape[dim] *= blocks.shape[0]
+    return jnp.moveaxis(blocks, 0, dim).reshape(shape)
 
 
 def normalize(values, frame_count, scaling, offsets):
@@ -99,7 +110,14 @@
     outgoing = jnp.where(
         sendable[None, None, :, None, None], jnp.take(pieces, source_tile, axis=2), 0
     )
-    received = lax.all_to_all(outgoing, "tile", split_axis=2, concat_axis=2, tiled=True)
+    size, here = (lax.axis_size("tile"), lax.axis_index("tile"))
+    tiles = split_up(outgoing, 2, size)
+    outs = [tiles[here]]
+    for step in range(1, size):
+        sent = tiles[here ^ step]
+        outs.append(lax.ppermute(sent, "tile", [(i, i ^ step) for i in range(size)]))
+    tiles = jnp.stack(outs)[here ^ jnp.arange(size)]
+    received = laid_out(tiles, 2)
     stacked = jnp.take(received, take_from, axis=2)
     block_out = convolve(stacked, conv_weight, conv_bias).astype(jnp.bfloat16)
     per_group = channels // GROUPS

time: 252 us -> 264 us (1.048)
  waiting for transfers between devices: 85.3 us -> 36.5 us
  starting transfers between devices: 7.56 us -> 44.2 us
  local copies, waits for them, and re-layouts: 37.9 us -> 67.2 us
    all_to_all x1 -> x0, waiting for transfers between devices: 85.3 us -> none  [local(): lax.all_to_all(outgoing, 'tile', split_axis=2, concat_axis=2, tiled=True)]
    ppermute x0 -> x15, starting transfers between devices: none -> 44.2 us  [local(): lax.ppermute(sent, 'tile', [(i, i ^ step) for i in range(size)])]
    ppermute x0 -> x15, waiting for transfers between devices: none -> 36.5 us  [local(): lax.ppermute(sent, 'tile', [(i, i ^ step) for i in range(size)])]
    unnamed x42 -> x67, local copies, waits for them, and re-layouts: 1.22 us -> 20.6 us
    all_to_all x1 -> x0, starting transfers between devices: 7.56 us -> none  [local(): lax.all_to_all(outgoing, 'tile', split_axis=2, concat_axis=2, tiled=True)]
    gather x0 -> x1, local copies, waits for them, and re-layouts: none -> 5.31 us  [local(): tiles = jnp.stack(outs)[here ^ jnp.arange(size)]]
    transpose x0 -> x1, local copies, waits for them, and re-layouts: none -> 5.02 us  [laid_out(): return jnp.moveaxis(blocks, 0, dim).reshape(shape)]
    all_to_all x1 -> x0, local copies, waits for them, and re-layouts: 4.91 us -> none  [local(): lax.all_to_all(outgoing, 'tile', split_axis=2, concat_axis=2, tiled=True)]
  transfers between devices with their start and end apart: 1 -> 15, of which waited for: 1 -> 5; matrix products, arithmetic and copies ran while one was open for 1% -> 8% of each run, Pallas kernels for 0% -> 0%
where the time goes in v1:
time: 264 us; the launch traced here: 263 us
  blocking collectives  75.2 us (28%)
  local copies, waits for them, and re-layouts  67.2 us (25%)
  starting transfers between devices  44.2 us (17%)
  waiting for transfers between devices  36.5 us (14%)
  other arithmetic  31.6 us (12%)
  matrix products  5.76 us (2%)
  between operations  2.66 us (1%)
    psum x1, blocking collectives, local(): lax.psum((jnp.dot(belongs.T, first_sum, precision=lax.Precision.HIGHEST),...  75.2 us
    ppermute x15, starting transfers between devices, local(): lax.ppermute(sent, 'tile', [(i, i ^ step) for i in range(size)])  44.2 us
    ppermute x15, waiting for transfers between devices, local(): lax.ppermute(sent, 'tile', [(i, i ^ step) for i in range(size)])  36.5 us
    unnamed x67, local copies, waits for them, and re-layouts  20.6 us
    gather x2, local copies, waits for them, and re-layouts, local(): jnp.take(pieces, source_tile, axis=2)  10.7 us
    convert_element_type x1, local copies, waits for them, and re-layouts, local(): block_out.astype(jnp.float32)  7 us
    gather x1, local copies, waits for them, and re-layouts, local(): tiles = jnp.stack(outs)[here ^ jnp.arange(size)]  5.31 us
  transfers between devices with their start and end apart: 15, of which 5 were waited for; matrix products, arithmetic and copies ran while one was open for 8% of the time, Pallas kernels for 0%

profile of v1, /device:TPU:0, one launch (start us, length us, event | category | flops | bytes accessed | tf_op | source)
XLA Modules:
  0.0 263.1 jit_solution(8258598755422816899)
XLA Ops:
  0.6 1.0 select_reduce_fusion.2
  2.4 1.9 fusion.38
  5.6 1.2 fusion.44
  6.8 1.2 compare_and_fusion
  8.7 2.3 fusion.11
  11.7 1.4 reduce_sum.116
  14.6 1.3 add_rsqrt_fusion
  18.0 1.7 fusion.9
  20.6 3.4 %maximum_maximum_fusion = bf16[3,4,96,8,256]{4,3,2,1,0:T(8,128)(2,1)} fusion(bf16[1,1,96,8,256]{4,3,2,1,0:T(8,128)(2,1)S(1)} %bitcast.142, bf16[1,1,96,8,256]{4,3,2,1,0:T(8,128)(2,1)S(1)} %bitcast.143, bf16[1,1,96,8,256]{4,3,2,1,0:T(8,128)(2,1)S(1)} %bitcast.144, bf16[1,1,96,8,256]{4,3,2,1,0:T(8,128)(2,1)S(1)} %bitcast.141, ...), kind=kLoop, calls=%fused_computation.22 | loop fusion | flops 25952256 | bytes 9437184 | tf_op jit(solution)/shard_map/stack | solution.py:109
  24.0 5.8 %gather_fusion = bf16[96,3,4,8,256]{4,3,2,1,0:T(8,128)(2,1)} fusion(bf16[3,4,96,8,256]{4,3,2,1,0:T(8,128)(2,1)} %maximum_maximum_fusion, s32[1024]{0:T(1024)S(1)} %pad_clamp_fusion.2), kind=kCustom, calls=%fused_computation | custom fusion | bytes 9437568 | tf_op jit(solution)/shard_map/jit(_take)/gather | solution.py:111
  29.8 4.9 %copy.149 = bf16[3,4,96,8,256]{4,3,2,1,0:T(8,128)(2,1)} copy(bf16[3,4,96,8,256]{4,3,1,0,2:T(8,128)(2,1)} %bitcast.134) | data formatting | bytes 9437184 | tf_op jit(solution)/shard_map/jit(_take)/gather | solution.py:111
  35.5 3.1 %select_select_fusion = bf16[3,4,16,6,8,256]{5,4,3,2,1,0:T(8,128)(2,1)S(1)} fusion(bf16[3,4,16,6,8,256]{5,4,3,2,1,0:T(8,128)(2,1)} %bitcast.133, pred[16,6]{1,0:T(8,128)(4,1)S(1)} %copy-done.5, pred[16,6]{1,0:T(8,128)(4,1)S(1)} %broadcast_compare_fusion), kind=kLoop, calls=%fused_computation.23 | loop fusion | flops 4718592 | bytes 9437376 | tf_op jit(solution)/shard_map/jit(_where)/select_n | solution.py:110
  38.6 2.1 copy-done.1
  40.7 2.2 dynamic-slice_bitcast_fusion
  43.3 2.5 collective-permute-start.1
  46.0 1.8 collective-permute-start.3
  49.0 1.8 bitcast_dynamic-update-slice_fusion.15
  51.4 1.2 convert_multiply_fusion.2
  52.7 2.6 %collective-permute-start.5 = (bf16[3,4,6,8,256]{4,3,2,1,0:T(8,128)(2,1)}, bf16[3,4,6,8,256]{4,3,2,1,0:T(8,128)(2,1)S(1)}, u32[]{:S(2)}, u32[]{:S(2)}) collective-permute-start(bf16[3,4,6,8,256]{4,3,2,1,0:T(8,128)(2,1)} %get-tuple-element.23), channel_id=1, source_target_pairs={{0,6},{1,7},{2,4},{3,5},{4,2},{5,3},{6,0},{7,1},{8,14},{9,15},{10,... | collective-permute-start | bytes 884744 | tf_op jit(solution)/shard_map/ppermute | solution.py:118
  55.3 1.7 bitcast_dynamic-update-slice_fusion.14
  57.1 1.7 bitcast_dynamic-update-slice_fusion.13
  58.8 1.1 collective-permute-done.2
  59.9 2.6 collective-permute-start.7
  62.6 1.7 bitcast_dynamic-update-slice_fusion.12
  64.4 1.7 bitcast_dynamic-update-slice_fusion.11
  66.1 3.6 %collective-permute-start.9 = (bf16[3,4,6,8,256]{4,3,2,1,0:T(8,128)(2,1)}, bf16[3,4,6,8,256]{4,3,2,1,0:T(8,128)(2,1)S(1)}, u32[]{:S(2)}, u32[]{:S(2)}) collective-permute-start(bf16[3,4,6,8,256]{4,3,2,1,0:T(8,128)(2,1)} %get-tuple-element.19), channel_id=1, source_target_pairs={{0,10},{1,11},{2,8},{3,9},{4,14},{5,15},{6,12},{7,13},{8,2},{9,3},... | collective-permute-start | bytes 884744 | tf_op jit(solution)/shard_map/ppermute | solution.py:118
  69.7 1.7 bitcast_dynamic-update-slice_fusion.10
  71.3 10.9 %collective-permute-done.5 = bf16[3,4,6,8,256]{4,3,2,1,0:T(8,128)(2,1)S(1)} collective-permute-done((bf16[3,4,6,8,256]{4,3,2,1,0:T(8,128)(2,1)}, bf16[3,4,6,8,256]{4,3,2,1,0:T(8,128)(2,1)S(1)}, u32[]{:S(2)}, u32[]{:S(2)}) %collective-permute-start.5) | collective-permute-done | bytes 294944 | tf_op jit(solution)/shard_map/ppermute | solution.py:118
  83.0 4.3 %collective-permute-done.6 = bf16[3,4,6,8,256]{4,3,2,1,0:T(8,128)(2,1)S(1)} collective-permute-done((bf16[3,4,6,8,256]{4,3,2,1,0:T(8,128)(2,1)}, bf16[3,4,6,8,256]{4,3,2,1,0:T(8,128)(2,1)S(1)}, u32[]{:S(2)}, u32[]{:S(2)}) %collective-permute-start.6) | collective-permute-done | bytes 294944 | tf_op jit(solution)/shard_map/ppermute | solution.py:118
  87.2 1.4 collective-permute-start.11
  89.4 2.3 collective-permute-start.12
  92.4 26.6 %collective-permute-start.13 = (bf16[3,4,6,8,256]{4,3,2,1,0:T(8,128)(2,1)S(1)}, bf16[3,4,6,8,256]{4,3,2,1,0:T(8,128)(2,1)S(1)}, u32[]{:S(2)}, u32[]{:S(2)}) collective-permute-start(bf16[3,4,6,8,256]{4,3,2,1,0:T(8,128)(2,1)S(1)} %copy-done.3), channel_id=1, source_target_pairs={{0,14},{1,15},{2,12},{3,13},{4,10},{5,11},{6,8},{7,9},{8,6},{9,7},... | collective-permute-start | bytes 884744 | tf_op jit(solution)/shard_map/ppermute | solution.py:118
  119.7 9.1 %collective-permute-done.9 = bf16[3,4,6,8,256]{4,3,2,1,0:T(8,128)(2,1)S(1)} collective-permute-done((bf16[3,4,6,8,256]{4,3,2,1,0:T(8,128)(2,1)}, bf16[3,4,6,8,256]{4,3,2,1,0:T(8,128)(2,1)S(1)}, u32[]{:S(2)}, u32[]{:S(2)}) %collective-permute-start.9) | collective-permute-done | bytes 294944 | tf_op jit(solution)/shard_map/ppermute | solution.py:118
  129.5 11.1 %collective-permute-done.10 = bf16[3,4,6,8,256]{4,3,2,1,0:T(8,128)(2,1)S(1)} collective-permute-done((bf16[3,4,6,8,256]{4,3,2,1,0:T(8,128)(2,1)}, bf16[3,4,6,8,256]{4,3,2,1,0:T(8,128)(2,1)S(1)}, u32[]{:S(2)}, u32[]{:S(2)}) %collective-permute-start.10) | collective-permute-done | bytes 294944 | tf_op jit(solution)/shard_map/ppermute | solution.py:118
  144.5 5.3 %gather_fusion.1 = bf16[16,3,4,6,8,256]{5,4,3,2,1,0:T(8,128)(2,1)} fusion(bf16[16,3,4,6,8,256]{5,4,3,2,1,0:T(8,128)(2,1)} %bitcast_dynamic-update-slice_fusion, s32[1024]{0:T(1024)S(1)} %pad_clamp_fusion.1), kind=kCustom, calls=%fused_computation.1 | custom fusion | bytes 9437248 | tf_op jit(solution)/shard_map/gather | solution.py:119
  149.8 5.0 %copy.150 = bf16[3,4,16,6,8,256]{5,4,3,2,1,0:T(8,128)(2,1)} copy(bf16[3,4,16,6,8,256]{5,4,3,1,0,2:T(8,128)(2,1)} %bitcast.135) | data formatting | bytes 9437184 | tf_op jit(solution)/shard_map/transpose | solution.py:20
  154.8 4.2 %gather_fusion.2 = bf16[32,3,4,8,256]{4,3,2,1,0:T(8,128)(2,1)} fusion(bf16[3,4,96,8,256]{4,3,2,1,0:T(8,128)(2,1)} %bitcast.136, s32[1024]{0:T(1024)S(1)} %pad_clamp_fusion), kind=kCustom, calls=%fused_computation.2 | custom fusion | bytes 3145856 | tf_op jit(solution)/shard_map/jit(_take)/gather | solution.py:121
  159.0 1.6 select_bitcast_fusion
  160.9 1.2 pad_slice_fusion
  163.7 2.7 %fusion.12 = bf16[512,256]{1,0:T(8,128)(2,1)} fusion(bf16[512,6912]{1,0:T(8,128)(2,1)S(1)} %constant_dynamic-update-slice_fusion, bf16[6912,256]{1,0:T(8,128)(2,1)S(1)} %bitcast.132, f32[256]{0:T(256)S(1)} %copy-done.12), kind=kOutput, calls=%fused_computation.41 | convolution fusion | flops 1812201472 | bytes 10880000 | tf_op jit(solution)/shard_map/dot_general | solution.py:52
  166.4 7.0 %reshape.467 = f32[2,32,8,32,8]{4,3,2,1,0:T(8,128)} reshape(bf16[512,256]{1,0:T(8,128)(2,1)} %fusion.12) | data formatting | bytes 786432 | tf_op jit(solution)/shard_map/convert_element_type | solution.py:124
  173.4 5.0 %fusion.48 = (f32[32,32]{1,0:T(8,128)S(1)}, f32[32,32]{1,0:T(8,128)S(1)}) fusion(f32[2,32,8,32,8]{4,3,2,1,0:T(8,128)} %reshape.467), kind=kLoop, calls=%fused_computation.194 | loop fusion | flops 391168 | bytes 532480 | tf_op jit(solution)/shard_map/reduce_sum | solution.py:127
  179.6 75.2 %all-reduce.2 = (f32[16,32]{1,0:T(8,128)}, f32[16,32]{1,0:T(8,128)}) all-reduce(f32[16,32]{1,0:T(8,128)S(1)} %fusion.14, f32[16,32]{1,0:T(8,128)S(1)} %fusion.16), channel_id=1, replica_groups=mesh['grp'=2,'tile'=16] {'tile'}, use_global_device_ids=true, to_apply=%region_14.15 | all-reduce | flops 1024 | bytes 8192 | tf_op jit(solution)/shard_map/psum | solution.py:130
  254.8 1.0 fusion.15
  256.4 1.6 copy.179
  258.0 1.0 fusion.13
  259.7 1.6 copy.181
  261.2 1.9 multiply_convert_fusion
  (137 shorter events, 21.5 us)
Async XLA Ops:
  0.6 162.9 %copy-start = (bf16[3,3,3,256,256]{4,3,2,1,0:T(8,128)(2,1)S(1)}, bf16[3,3,3,256,256]{4,3,2,1,0:T(8,128)(2,1)}, u32[]{:S(2)}) copy-start(bf16[3,3,3,256,256]{4,3,2,1,0:T(8,128)(2,1)} %param.14) | copy-start | bytes 10616836
  1.7 0.5 copy-start.9
  19.9 0.7 copy-start.11
  29.8 5.7 %copy-start.5 = (pred[16,6]{1,0:T(8,128)(4,1)S(1)}, pred[16,6]{1,0:T(8,128)(4,1)}, u32[]{:S(2)}) copy-start(pred[16,6]{1,0:T(8,128)(4,1)} %compare_and_fusion) | copy-start | bytes 292
  38.6 2.1 copy-start.1
  40.7 7.6 %copy-start.8 = (s32[16]{0:T(128)S(1)}, s32[16]{0:T(128)}, u32[]{:S(2)}) copy-start(s32[16]{0:T(128)} %get-tuple-element.11) | copy-start | bytes 196
  40.7 7.7 %copy-start.7 = (s32[16]{0:T(128)S(1)}, s32[16]{0:T(128)}, u32[]{:S(2)}) copy-start(s32[16]{0:T(128)} %param.11) | copy-start | bytes 196
  42.9 9.8 %collective-permute-start = (bf16[3,4,6,8,256]{4,3,2,1,0:T(8,128)(2,1)}, bf16[3,4,6,8,256]{4,3,2,1,0:T(8,128)(2,1)}, u32[]{:S(2)}, u32[]{:S(2)}) collective-permute-start(bf16[3,4,6,8,256]{4,3,2,1,0:T(8,128)(2,1)} %get-tuple-element.28), channel_id=1, source_target_pairs={{0,1},{1,0},{2,3},{3,2},{4,5},{5,4},{6,7},{7,6},{8,9},{9,8},{10,11... | collective-permute-start | bytes 884744 | tf_op jit(solution)/shard_map/ppermute | solution.py:118
  43.3 13.7 %collective-permute-start.1 = (bf16[3,4,6,8,256]{4,3,2,1,0:T(8,128)(2,1)}, bf16[3,4,6,8,256]{4,3,2,1,0:T(8,128)(2,1)}, u32[]{:S(2)}, u32[]{:S(2)}) collective-permute-start(bf16[3,4,6,8,256]{4,3,2,1,0:T(8,128)(2,1)} %get-tuple-element.27), channel_id=1, source_target_pairs={{0,2},{1,3},{2,0},{3,1},{4,6},{5,7},{6,4},{7,5},{8,10},{9,11},{10,... | collective-permute-start | bytes 884744 | tf_op jit(solution)/shard_map/ppermute | solution.py:118
  45.8 14.1 %collective-permute-start.2 = (bf16[3,4,6,8,256]{4,3,2,1,0:T(8,128)(2,1)}, bf16[3,4,6,8,256]{4,3,2,1,0:T(8,128)(2,1)}, u32[]{:S(2)}, u32[]{:S(2)}) collective-permute-start(bf16[3,4,6,8,256]{4,3,2,1,0:T(8,128)(2,1)} %get-tuple-element.26), channel_id=1, source_target_pairs={{0,3},{1,2},{2,1},{3,0},{4,7},{5,6},{6,5},{7,4},{8,11},{9,10},{10,... | collective-permute-start | bytes 884744 | tf_op jit(solution)/shard_map/ppermute | solution.py:118
  46.0 18.3 %collective-permute-start.3 = (bf16[3,4,6,8,256]{4,3,2,1,0:T(8,128)(2,1)}, bf16[3,4,6,8,256]{4,3,2,1,0:T(8,128)(2,1)}, u32[]{:S(2)}, u32[]{:S(2)}) collective-permute-start(bf16[3,4,6,8,256]{4,3,2,1,0:T(8,128)(2,1)} %get-tuple-element.25), channel_id=1, source_target_pairs={{0,4},{1,5},{2,6},{3,7},{4,0},{5,1},{6,2},{7,3},{8,12},{9,13},{10,... | collective-permute-start | bytes 884744 | tf_op jit(solution)/shard_map/ppermute | solution.py:118
  47.7 18.3 %collective-permute-start.4 = (bf16[3,4,6,8,256]{4,3,2,1,0:T(8,128)(2,1)}, bf16[3,4,6,8,256]{4,3,2,1,0:T(8,128)(2,1)}, u32[]{:S(2)}, u32[]{:S(2)}) collective-permute-start(bf16[3,4,6,8,256]{4,3,2,1,0:T(8,128)(2,1)} %get-tuple-element.24), channel_id=1, source_target_pairs={{0,5},{1,4},{2,7},{3,6},{4,1},{5,0},{6,3},{7,2},{8,13},{9,12},{10,... | collective-permute-start | bytes 884744 | tf_op jit(solution)/shard_map/ppermute | solution.py:118
  48.5 130.0 %copy-start.6 = (s32[32]{0:T(128)}, s32[32]{0:T(128)S(1)}, u32[]{:S(2)}) copy-start(s32[32]{0:T(128)S(1)} %get-tuple-element.6) | copy-start | bytes 388
  49.0 40.4 %copy-start.4 = (bf16[3,4,6,8,256]{4,3,2,1,0:T(8,128)(2,1)S(1)}, bf16[3,4,6,8,256]{4,3,2,1,0:T(8,128)(2,1)}, u32[]{:S(2)}) copy-start(bf16[3,4,6,8,256]{4,3,2,1,0:T(8,128)(2,1)} %get-tuple-element.16) | copy-start | bytes 884740
  49.0 43.4 %copy-start.3 = (bf16[3,4,6,8,256]{4,3,2,1,0:T(8,128)(2,1)S(1)}, bf16[3,4,6,8,256]{4,3,2,1,0:T(8,128)(2,1)}, u32[]{:S(2)}) copy-start(bf16[3,4,6,8,256]{4,3,2,1,0:T(8,128)(2,1)} %get-tuple-element.15) | copy-start | bytes 884740
  49.0 79.8 %copy-start.2 = (bf16[3,4,6,8,256]{4,3,2,1,0:T(8,128)(2,1)S(1)}, bf16[3,4,6,8,256]{4,3,2,1,0:T(8,128)(2,1)}, u32[]{:S(2)}) copy-start(bf16[3,4,6,8,256]{4,3,2,1,0:T(8,128)(2,1)} %get-tuple-element.14) | copy-start | bytes 884740
  52.7 29.6 %collective-permute-start.5 = (bf16[3,4,6,8,256]{4,3,2,1,0:T(8,128)(2,1)}, bf16[3,4,6,8,256]{4,3,2,1,0:T(8,128)(2,1)S(1)}, u32[]{:S(2)}, u32[]{:S(2)}) collective-permute-start(bf16[3,4,6,8,256]{4,3,2,1,0:T(8,128)(2,1)} %get-tuple-element.23), channel_id=1, source_target_pairs={{0,6},{1,7},{2,4},{3,5},{4,2},{5,3},{6,0},{7,1},{8,14},{9,15},{10,... | collective-permute-start | bytes 884744 | tf_op jit(solution)/shard_map/ppermute | solution.py:118
  57.0 30.2 %collective-permute-start.6 = (bf16[3,4,6,8,256]{4,3,2,1,0:T(8,128)(2,1)}, bf16[3,4,6,8,256]{4,3,2,1,0:T(8,128)(2,1)S(1)}, u32[]{:S(2)}, u32[]{:S(2)}) collective-permute-start(bf16[3,4,6,8,256]{4,3,2,1,0:T(8,128)(2,1)} %get-tuple-element.22), channel_id=1, source_target_pairs={{0,7},{1,6},{2,5},{3,4},{4,3},{5,2},{6,1},{7,0},{8,15},{9,14},{10,... | collective-permute-start | bytes 884744 | tf_op jit(solution)/shard_map/ppermute | solution.py:118
  59.9 29.4 %collective-permute-start.7 = (bf16[3,4,6,8,256]{4,3,2,1,0:T(8,128)(2,1)}, bf16[3,4,6,8,256]{4,3,2,1,0:T(8,128)(2,1)S(1)}, u32[]{:S(2)}, u32[]{:S(2)}) collective-permute-start(bf16[3,4,6,8,256]{4,3,2,1,0:T(8,128)(2,1)} %get-tuple-element.21), channel_id=1, source_target_pairs={{0,8},{1,9},{2,10},{3,11},{4,12},{5,13},{6,14},{7,15},{8,0},{9,1},... | collective-permute-start | bytes 884744 | tf_op jit(solution)/shard_map/ppermute | solution.py:118
  64.3 28.1 %collective-permute-start.8 = (bf16[3,4,6,8,256]{4,3,2,1,0:T(8,128)(2,1)}, bf16[3,4,6,8,256]{4,3,2,1,0:T(8,128)(2,1)S(1)}, u32[]{:S(2)}, u32[]{:S(2)}) collective-permute-start(bf16[3,4,6,8,256]{4,3,2,1,0:T(8,128)(2,1)} %get-tuple-element.20), channel_id=1, source_target_pairs={{0,9},{1,8},{2,11},{3,10},{4,13},{5,12},{6,15},{7,14},{8,1},{9,0},... | collective-permute-start | bytes 884744 | tf_op jit(solution)/shard_map/ppermute | solution.py:118
  66.1 62.7 %collective-permute-start.9 = (bf16[3,4,6,8,256]{4,3,2,1,0:T(8,128)(2,1)}, bf16[3,4,6,8,256]{4,3,2,1,0:T(8,128)(2,1)S(1)}, u32[]{:S(2)}, u32[]{:S(2)}) collective-permute-start(bf16[3,4,6,8,256]{4,3,2,1,0:T(8,128)(2,1)} %get-tuple-element.19), channel_id=1, source_target_pairs={{0,10},{1,11},{2,8},{3,9},{4,14},{5,15},{6,12},{7,13},{8,2},{9,3},... | collective-permute-start | bytes 884744 | tf_op jit(solution)/shard_map/ppermute | solution.py:118
  82.2 58.4 %collective-permute-start.10 = (bf16[3,4,6,8,256]{4,3,2,1,0:T(8,128)(2,1)}, bf16[3,4,6,8,256]{4,3,2,1,0:T(8,128)(2,1)S(1)}, u32[]{:S(2)}, u32[]{:S(2)}) collective-permute-start(bf16[3,4,6,8,256]{4,3,2,1,0:T(8,128)(2,1)} %get-tuple-element.18), channel_id=1, source_target_pairs={{0,11},{1,10},{2,9},{3,8},{4,15},{5,14},{6,13},{7,12},{8,3},{9,2},... | collective-permute-start | bytes 884744 | tf_op jit(solution)/shard_map/ppermute | solution.py:118
  87.2 54.1 %collective-permute-start.11 = (bf16[3,4,6,8,256]{4,3,2,1,0:T(8,128)(2,1)}, bf16[3,4,6,8,256]{4,3,2,1,0:T(8,128)(2,1)S(1)}, u32[]{:S(2)}, u32[]{:S(2)}) collective-permute-start(bf16[3,4,6,8,256]{4,3,2,1,0:T(8,128)(2,1)} %get-tuple-element.17), channel_id=1, source_target_pairs={{0,12},{1,13},{2,14},{3,15},{4,8},{5,9},{6,10},{7,11},{8,4},{9,5},... | collective-permute-start | bytes 884744 | tf_op jit(solution)/shard_map/ppermute | solution.py:118
  89.4 52.8 %collective-permute-start.12 = (bf16[3,4,6,8,256]{4,3,2,1,0:T(8,128)(2,1)S(1)}, bf16[3,4,6,8,256]{4,3,2,1,0:T(8,128)(2,1)S(1)}, u32[]{:S(2)}, u32[]{:S(2)}) collective-permute-start(bf16[3,4,6,8,256]{4,3,2,1,0:T(8,128)(2,1)S(1)} %copy-done.4), channel_id=1, source_target_pairs={{0,13},{1,12},{2,15},{3,14},{4,9},{5,8},{6,11},{7,10},{8,5},{9,4},... | collective-permute-start | bytes 884744 | tf_op jit(solution)/shard_map/ppermute | solution.py:118
  92.4 50.5 %collective-permute-start.13 = (bf16[3,4,6,8,256]{4,3,2,1,0:T(8,128)(2,1)S(1)}, bf16[3,4,6,8,256]{4,3,2,1,0:T(8,128)(2,1)S(1)}, u32[]{:S(2)}, u32[]{:S(2)}) collective-permute-start(bf16[3,4,6,8,256]{4,3,2,1,0:T(8,128)(2,1)S(1)} %copy-done.3), channel_id=1, source_target_pairs={{0,14},{1,15},{2,12},{3,13},{4,10},{5,11},{6,8},{7,9},{8,6},{9,7},... | collective-permute-start | bytes 884744 | tf_op jit(solution)/shard_map/ppermute | solution.py:118
  128.8 14.9 %collective-permute-start.14 = (bf16[3,4,6,8,256]{4,3,2,1,0:T(8,128)(2,1)S(1)}, bf16[3,4,6,8,256]{4,3,2,1,0:T(8,128)(2,1)S(1)}, u32[]{:S(2)}, u32[]{:S(2)}) collective-permute-start(bf16[3,4,6,8,256]{4,3,2,1,0:T(8,128)(2,1)S(1)} %copy-done.2), channel_id=1, source_target_pairs={{0,15},{1,14},{2,13},{3,12},{4,11},{5,10},{6,9},{7,8},{8,7},{9,6},... | collective-permute-start | bytes 884744 | tf_op jit(solution)/shard_map/ppermute | solution.py:118
  149.8 9.3 %copy-start.10 = (pred[32]{0:T(512)(128)(4,1)S(1)}, pred[32]{0:T(512)(128)(4,1)}, u32[]{:S(2)}) copy-start(pred[32]{0:T(512)(128)(4,1)} %compare_and_fusion.1) | copy-start | bytes 100
  163.0 0.7 copy-start.12
